TPU v7x, 32 devices: a whole 2x2x4 slice. The times are simulated.
32 devices in a mesh: expert: 8 (over z, y), shard: 4 (over x, core).
Axes of the slice: x: 2, y: 2, z: 4, core: 2. Of those that a mesh axis runs over, the one named last changes fastest.
Arguments:
- tokens: float32 [25216, 512], P(('expert', 'shard')), may hold values from -6 to 6
- routes: int32 [25216, 2], P(('expert', 'shard')), may hold values from 0 to 7, all different within a row; in each aligned block of 394 rows (0 to 393, 394 to 787, ...) at most 192 rows name the same one
- priority: int32 [25216], P(('expert', 'shard')), may hold values from 0 to 393, as said below
- norm_gain: bfloat16 [2, 2, 512], P(None, None, 'shard'), may hold values from 0.5 to 1.5
- norm_bias: bfloat16 [2, 2, 512], P(None, None, 'shard'), may hold values from -1 to 1
- w_qkv: bfloat16 [2, 512, 1536], P(None, 'shard'), may hold values from -0.25 to 0.25
- w_proj: bfloat16 [2, 512, 512], P(None, 'shard'), may hold values from -2 to 2
- w_router: bfloat16 [2, 512, 8], P(None, 'shard'), may hold values from -0.1875 to 0.1875
- exp_in: bfloat16 [2, 8, 512, 2048], P(None, 'expert', 'shard'), may hold values from -0.25 to 0.25
- exp_out: bfloat16 [2, 8, 2048, 512], P(None, 'expert', 'shard'), may hold values from -0.875 to 0.875
- cotangent: float32 [25216, 512], P(('expert', 'shard')), may hold values from -6 to 6
Outputs:
- activations: float32 [25216, 512], P(('expert', 'shard'))
- d_tokens: float32 [25216, 512], P(('expert', 'shard'))
- grad_gain: float32 [2, 2, 512], P(None, None, 'shard')
- grad_bias: float32 [2, 2, 512], P(None, None, 'shard')
- grad_qkv: float32 [2, 512, 1536], P(None, 'shard')
- grad_proj: float32 [2, 512, 512], P(None, 'shard')
- grad_router: float32 [2, 512, 8], P(None, 'shard')
- grad_exp_in: float32 [2, 8, 512, 2048], P(None, 'expert', 'shard')
- grad_exp_out: float32 [2, 8, 2048, 512], P(None, 'expert', 'shard')
Inputs may be any that keep to these rules, and one draw needn't show every extreme that they name: `routes`: each row names 2 different experts; in each aligned block of 394 rows no expert is named by more than 192 rows. `priority`: in each aligned block of 394 rows the values are a permutation of 0 to 393.
All inputs are finite; a program needn't handle non-finite values.
Results may differ from a plain program's by a relative error of at most 0.025.
Values may be sent and summed in bfloat16 or wider, within the bound.
No kernel may reach another device: no remote copies, remote signals or barrier semaphores. Data moves between devices by JAX's collectives and lax.ppermute only.
A program may use at most 256 MiB of HBM per device.

v0:
```python
import jax
import jax.numpy as jnp
from jax import lax
from jax.sharding import PartitionSpec as P

D = 512
HEADS = 8
HEAD = 64
HIDDEN_SIZE = 2048
EXP_DEV = 1
SEQ = 197
MICRO = 2
LAYERS = 2
TOP = 2
TOK_MB = 394
norm_eps = 1e-06


def layer_norm(values, norm_scale, norm_shift):
    centre = values - jnp.mean(values, axis=-1, keepdims=True)
    spread = jnp.mean(centre * centre, axis=-1, keepdims=True)
    return centre * lax.rsqrt(spread + norm_eps) * norm_scale + norm_shift


def gelu_tanh(values):
    return jax.nn.gelu(values, approximate=True)


def dot_first(left, right):
    return lax.dot_general(
        left, right, (((0,), (0,)), ((), ())), preferred_element_type=jnp.float32
    )


def dot_last(left, right):
    return lax.dot_general(
        left, right, (((1,), (1,)), ((), ())), preferred_element_type=jnp.float32
    )


def slot_tables(route_ids, prio_rank, experts, capacity):
    tok_count = route_ids.shape[0]
    order_key = jnp.concatenate([prio_rank, prio_rank + tok_count])
    pair_expert = jnp.concatenate([route_ids[:, 0], route_ids[:, 1]])
    same_expert = pair_expert[:, None] == pair_expert[None, :]
    earlier = order_key[None, :] < order_key[:, None]
    position = jnp.sum((same_expert & earlier).astype(jnp.int32), axis=1)
    kept_mask = position < capacity
    flat_slot = jnp.where(kept_mask, pair_expert * capacity + position, experts * capacity)
    pair_ids = jnp.arange(2 * tok_count, dtype=jnp.int32)
    slot_pair = (
        jnp.full((experts * capacity + 1,), 2 * tok_count, jnp.int32).at[flat_slot].set(pair_ids)
    )
    slot_pair = slot_pair[: experts * capacity]
    slot_token = jnp.where(slot_pair < 2 * tok_count, slot_pair % tok_count, tok_count)
    return (flat_slot, slot_pair, slot_token, kept_mask)


def forward_layer(residual, route_ids, prio_rank, weights, experts, capacity):
    norm_gains, norm_shifts, qkv_w, proj_w, router_w, in_w, out_w = weights
    tok_count = residual.shape[0]
    seq_count = tok_count // SEQ
    score_scale = HEAD ** (-0.5)
    norm_scale = norm_gains.astype(jnp.float32)
    norm_shift = norm_shifts.astype(jnp.float32)
    normed = layer_norm(residual, norm_scale[0], norm_shift[0]).astype(jnp.bfloat16)
    qkv_rows = jnp.dot(normed, qkv_w, preferred_element_type=jnp.float32).astype(jnp.bfloat16)
    heads = qkv_rows.reshape(seq_count, SEQ, 3, HEADS, HEAD)
    scores = (
        jnp.einsum(
            "sqhd,skhd->shqk", heads[:, :, 0], heads[:, :, 1], preferred_element_type=jnp.float32
        )
        * score_scale
    )
    row_top = jnp.max(scores, axis=-1, keepdims=True)
    scores_exp = jnp.exp(scores - row_top)
    row_total = jnp.sum(scores_exp, axis=-1, keepdims=True)
    soft_scores = scores_exp / row_total
    log_total = row_top + jnp.log(row_total)
    mixed_heads = jnp.einsum(
        "shqk,skhd->sqhd",
        soft_scores.astype(jnp.bfloat16),
        heads[:, :, 2],
        preferred_element_type=jnp.float32,
    )
    mixed_heads = mixed_heads.astype(jnp.bfloat16).reshape(tok_count, D)
    middle = residual + jnp.dot(mixed_heads, proj_w, preferred_element_type=jnp.float32)
    normed_two = layer_norm(middle, norm_scale[1], norm_shift[1]).astype(jnp.bfloat16)
    gate_probs = jax.nn.softmax(
        jnp.dot(normed_two, router_w, preferred_element_type=jnp.float32), axis=-1
    )
    flat_slot, slot_pair, slot_token, kept_mask = slot_tables(
        route_ids, prio_rank, experts, capacity
    )
    padded = jnp.concatenate([normed_two, jnp.zeros((1, D), jnp.bfloat16)])
    sending = padded[slot_token].reshape(experts, capacity, D)
    received = lax.all_to_all(sending, "expert", split_axis=0, concat_axis=0, tiled=True)
    sources = received.shape[0]
    item_count = received.shape[1]
    row_block = received.reshape(sources * item_count, D)
    hidden_pre = jnp.dot(row_block, in_w[0], preferred_element_type=jnp.float32)
    hidden_act = gelu_tanh(hidden_pre).astype(jnp.bfloat16)
    expert_rows = jnp.dot(hidden_act, out_w[0], preferred_element_type=jnp.float32).astype(
        jnp.bfloat16
    )
    returned = lax.all_to_all(
        expert_rows.reshape(sources, item_count, D),
        "expert",
        split_axis=0,
        concat_axis=0,
        tiled=True,
    )
    returned, received, hidden_pre = (
        returned,
        received,
        hidden_pre.reshape(sources, item_count, HIDDEN_SIZE),
    )
    back_rows = jnp.concatenate(
        [returned.reshape(experts * capacity, D), jnp.zeros((1, D), jnp.bfloat16)]
    )
    pair_rows = back_rows[flat_slot].astype(jnp.float32).reshape(TOP, tok_count, D)
    route_hot = (
        route_ids[:, :, None] == jnp.arange(experts, dtype=jnp.int32)[None, None, :]
    ).astype(jnp.float32)
    chosen = jnp.sum(route_hot * gate_probs[:, None, :], axis=-1)
    kept_gate = kept_mask.astype(jnp.float32).reshape(TOP, tok_count)
    weight_pair = kept_gate * chosen.T
    combined = jnp.sum(weight_pair[:, :, None] * pair_rows, axis=0)
    output = middle + combined
    saved_state = (
        residual,
        normed,
        heads,
        log_total,
        mixed_heads,
        middle,
        normed_two,
        gate_probs,
        route_hot,
        kept_gate,
        weight_pair,
        flat_slot,
        slot_pair,
        pair_rows,
        received,
        hidden_pre,
    )
    return (output, saved_state)


def backward_layer(d_output, saved_state, weights, experts, capacity):
    (
        residual,
        normed,
        heads,
        log_total,
        mixed_heads,
        middle,
        normed_two,
        gate_probs,
        route_hot,
        kept_gate,
        weight_pair,
        flat_slot,
        slot_pair,
        pair_rows,
        received,
        hidden_pre,
    ) = saved_state
    norm_gains, norm_shifts, qkv_w, proj_w, router_w, in_w, out_w = weights
    tok_count = residual.shape[0]
    seq_count = tok_count // SEQ
    score_scale = HEAD ** (-0.5)
    norm_scale = norm_gains.astype(jnp.float32)
    norm_shift = norm_shifts.astype(jnp.float32)
    d_gate_pair = kept_gate * jnp.sum(d_output[None] * pair_rows, axis=-1)
    d_gates = jnp.sum(route_hot * d_gate_pair.T[:, :, None], axis=1)
    d_logits = (
        gate_probs * (d_gates - jnp.sum(gate_probs * d_gates, axis=-1, keepdims=True))
    ).astype(jnp.bfloat16)
    g_router = dot_first(normed_two, d_logits)
    d_normed_two = dot_last(d_logits, router_w)
    d_pairs = (
        (weight_pair[:, :, None] * d_output[None]).astype(jnp.bfloat16).reshape(TOP * tok_count, D)
    )
    d_slots = jnp.concatenate([d_pairs, jnp.zeros((1, D), jnp.bfloat16)])[slot_pair].reshape(
        experts, capacity, D
    )
    d_expert_out = lax.all_to_all(d_slots, "expert", split_axis=0, concat_axis=0, tiled=True)
    flat_out = d_expert_out.reshape(experts * capacity, D)
    hidden_flat = hidden_pre.reshape(experts * capacity, HIDDEN_SIZE)
    hidden_act = gelu_tanh(hidden_flat).astype(jnp.bfloat16)
    g_out = dot_first(hidden_act, flat_out)
    d_act = dot_last(flat_out, out_w[0])
    d_pre = jax.vjp(gelu_tanh, hidden_flat)[1](d_act)[0].astype(jnp.bfloat16)
    g_in = dot_first(received.reshape(experts * capacity, D), d_pre)
    d_rows = dot_last(d_pre, in_w[0]).astype(jnp.bfloat16).reshape(experts, capacity, D)
    d_back = lax.all_to_all(d_rows, "expert", split_axis=0, concat_axis=0, tiled=True)
    d_pair_in = jnp.concatenate(
        [d_back.reshape(experts * capacity, D), jnp.zeros((1, D), jnp.bfloat16)]
    )[flat_slot]
    d_pair_in = d_pair_in.astype(jnp.float32).reshape(TOP, tok_count, D)
    d_normed_two = d_normed_two + jnp.sum(d_pair_in, axis=0)
    pulled_two = jax.vjp(layer_norm, middle, norm_scale[1], norm_shift[1])[1](d_normed_two)
    d_middle = d_output + pulled_two[0]
    d_branch = d_middle.astype(jnp.bfloat16)
    g_proj = dot_first(mixed_heads, d_branch)
    d_mixed = dot_last(d_branch, proj_w).astype(jnp.bfloat16).reshape(seq_count, SEQ, HEADS, HEAD)
    query_heads = heads[:, :, 0]
    key_heads = heads[:, :, 1]
    value_heads = heads[:, :, 2]
    scores = (
        jnp.einsum("sqhd,skhd->shqk", query_heads, key_heads, preferred_element_type=jnp.float32)
        * score_scale
    )
    soft_scores = jnp.exp(scores - log_total)
    d_soft = jnp.einsum("sqhd,skhd->shqk", d_mixed, value_heads, preferred_element_type=jnp.float32)
    d_values = jnp.einsum(
        "shqk,sqhd->skhd",
        soft_scores.astype(jnp.bfloat16),
        d_mixed,
        preferred_element_type=jnp.float32,
    )
    d_scores = (
        soft_scores * (d_soft - jnp.sum(soft_scores * d_soft, axis=-1, keepdims=True))
    ).astype(jnp.bfloat16)
    d_query = (
        jnp.einsum("shqk,skhd->sqhd", d_scores, key_heads, preferred_element_type=jnp.float32)
        * score_scale
    )
    d_keys = (
        jnp.einsum("shqk,sqhd->skhd", d_scores, query_heads, preferred_element_type=jnp.float32)
        * score_scale
    )
    d_qkv = (
        jnp.stack([d_query, d_keys, d_values], axis=2)
        .reshape(tok_count, 3 * D)
        .astype(jnp.bfloat16)
    )
    g_qkv = dot_first(normed, d_qkv)
    d_normed = dot_last(d_qkv, qkv_w)
    pulled_one = jax.vjp(layer_norm, residual, norm_scale[0], norm_shift[0])[1](d_normed)
    d_residual = d_middle + pulled_one[0]
    g_gain = jnp.stack([pulled_one[1], pulled_two[1]])
    g_shift = jnp.stack([pulled_one[2], pulled_two[2]])
    return (d_residual, (g_gain, g_shift, g_qkv, g_proj, g_router, g_in[None], g_out[None]))


def local(
    tokens,
    routes,
    priority,
    norm_gain,
    norm_bias,
    w_qkv,
    w_proj,
    w_router,
    exp_in,
    exp_out,
    cotangent,
):
    experts = lax.axis_size("expert") * EXP_DEV
    capacity = max(8, (5 * TOK_MB // (2 * experts) + 7) // 8 * 8)
    totals = []
    for layer_index in range(LAYERS):
        totals.append(None)
    out_blocks = []
    grad_blocks = []
    for micro_index in range(MICRO):
        row_start = micro_index * TOK_MB
        residual = tokens[row_start : row_start + TOK_MB]
        route_ids = routes[row_start : row_start + TOK_MB]
        prio_rank = priority[row_start : row_start + TOK_MB]
        saved_list = []
        for layer_index in range(LAYERS):
            weights = (
                lax.all_gather(norm_gain[layer_index], "shard", axis=1, tiled=True),
                lax.all_gather(norm_bias[layer_index], "shard", axis=1, tiled=True),
                lax.all_gather(w_qkv[layer_index], "shard", axis=0, tiled=True),
                lax.all_gather(w_proj[layer_index], "shard", axis=0, tiled=True),
                lax.all_gather(w_router[layer_index], "shard", axis=0, tiled=True),
                lax.all_gather(exp_in[layer_index], "shard", axis=1, tiled=True),
                lax.all_gather(exp_out[layer_index], "shard", axis=1, tiled=True),
            )
            residual, saved_state = forward_layer(
                residual, route_ids, prio_rank, weights, experts, capacity
            )
            saved_list.append(saved_state)
        out_blocks.append(residual)
        d_residual = cotangent[row_start : row_start + TOK_MB]
        for layer_index in reversed(range(LAYERS)):
            weights = (
                lax.all_gather(norm_gain[layer_index], "shard", axis=1, tiled=True),
                lax.all_gather(norm_bias[layer_index], "shard", axis=1, tiled=True),
                lax.all_gather(w_qkv[layer_index], "shard", axis=0, tiled=True),
                lax.all_gather(w_proj[layer_index], "shard", axis=0, tiled=True),
                lax.all_gather(w_router[layer_index], "shard", axis=0, tiled=True),
                lax.all_gather(exp_in[layer_index], "shard", axis=1, tiled=True),
                lax.all_gather(exp_out[layer_index], "shard", axis=1, tiled=True),
            )
            d_residual, layer_grads = backward_layer(
                d_residual, saved_list[layer_index], weights, experts, capacity
            )
            if totals[layer_index] is None:
                totals[layer_index] = layer_grads
            else:
                totals[layer_index] = tuple(
                    (
                        old_sum + new_term
                        for old_sum, new_term in zip(totals[layer_index], layer_grads)
                    )
                )
        grad_blocks.append(d_residual)
    stacked = tuple(
        (
            jnp.stack([totals[layer_index][kind_index] for layer_index in range(LAYERS)])
            for kind_index in range(7)
        )
    )
    scattered = (
        lax.psum_scatter(
            stacked[0].astype(jnp.bfloat16), "shard", scatter_dimension=2, tiled=True
        ).astype(jnp.float32),
        lax.psum_scatter(
            stacked[1].astype(jnp.bfloat16), "shard", scatter_dimension=2, tiled=True
        ).astype(jnp.float32),
        lax.psum_scatter(
            stacked[2].astype(jnp.bfloat16), "shard", scatter_dimension=1, tiled=True
        ).astype(jnp.float32),
        lax.psum_scatter(
            stacked[3].astype(jnp.bfloat16), "shard", scatter_dimension=1, tiled=True
        ).astype(jnp.float32),
        lax.psum_scatter(
            stacked[4].astype(jnp.bfloat16), "shard", scatter_dimension=1, tiled=True
        ).astype(jnp.float32),
        lax.psum_scatter(
            stacked[5].astype(jnp.bfloat16), "shard", scatter_dimension=2, tiled=True
        ).astype(jnp.float32),
        lax.psum_scatter(
            stacked[6].astype(jnp.bfloat16), "shard", scatter_dimension=2, tiled=True
        ).astype(jnp.float32),
    )
    replicated = (
        lax.psum(scattered[0].astype(jnp.bfloat16), "expert").astype(jnp.float32),
        lax.psum(scattered[1].astype(jnp.bfloat16), "expert").astype(jnp.float32),
        lax.psum(scattered[2].astype(jnp.bfloat16), "expert").astype(jnp.float32),
        lax.psum(scattered[3].astype(jnp.bfloat16), "expert").astype(jnp.float32),
        lax.psum(scattered[4].astype(jnp.bfloat16), "expert").astype(jnp.float32),
    )
    activations = jnp.concatenate(out_blocks, axis=0)
    d_tokens = jnp.concatenate(grad_blocks, axis=0)
    return (
        activations,
        d_tokens,
        replicated[0],
        replicated[1],
        replicated[2],
        replicated[3],
        replicated[4],
        scattered[5],
        scattered[6],
    )


def solution(mesh):
    return jax.shard_map(
        local,
        mesh=mesh,
        in_specs=(
            P(("expert", "shard"), None),
            P(("expert", "shard"), None),
            P(("expert", "shard")),
            P(None, None, "shard"),
            P(None, None, "shard"),
            P(None, "shard", None),
            P(None, "shard", None),
            P(None, "shard", None),
            P(None, "expert", "shard", None),
            P(None, "expert", "shard", None),
            P(("expert", "shard"), None),
        ),
        out_specs=(
            P(("expert", "shard"), None),
            P(("expert", "shard"), None),
            P(None, None, "shard"),
            P(None, None, "shard"),
            P(None, "shard", None),
            P(None, "shard", None),
            P(None, "shard", None),
            P(None, "expert", "shard", None),
            P(None, "expert", "shard", None),
        ),
        check_vma=False,
    )
```

profile of v0, /device:TPU:0, one launch (start us, length us, event | category | flops | bytes accessed | tf_op | source)
XLA Modules:
  0.0 1039.3 jit_solution(6262433277946074067)
XLA Ops:
  14.2 6.0 all-gather
  20.3 5.5 all-gather.1
  26.5 8.2 all-gather.3
  35.8 5.3 scatter_custom_fusion.1
  87.3 5.5 gather_fusion.4
  92.8 5.6 all-to-all-start.4
  99.9 5.3 scatter_custom_fusion
  110.9 5.1 gather_fusion
  116.0 8.7 all-to-all-done.4
  129.0 7.2 all-gather.10
  141.8 7.6 fusion.80
  149.5 7.7 fusion.125
  157.2 5.9 all-to-all-start.5
  163.2 8.9 multiply_convert_fusion.3
  177.4 12.0 %all-to-all-done.5 = bf16[8,128,512]{2,1,0:T(8,128)(2,1)} async-done(((bf16[8,128,512]{2,1,0:T(8,128)(2,1)}), bf16[8,128,512]{2,1,0:T(8,128)(2,1)}, u32[]{:S(2)}, u32[]{:S(2)}) %all-to-all-start.5) | async-done | bytes 1048608 | tf_op jit(solution)/shard_map/all_to_all | solution.py:106
  193.9 5.2 all-gather.4
  207.8 11.5 %all-to-all-done.1 = bf16[8,128,512]{2,1,0:T(8,128)(2,1)} async-done(((bf16[8,128,512]{2,1,0:T(8,128)(2,1)}), bf16[8,128,512]{2,1,0:T(8,128)(2,1)}, u32[]{:S(2)}, u32[]{:S(2)}) %all-to-all-start.1) | async-done | bytes 1048608 | tf_op jit(solution)/shard_map/all_to_all | solution.py:106
  269.3 5.1 gather_fusion.2
  285.1 5.2 all-gather.11
  293.4 5.1 gather_fusion.8
  298.5 5.6 all-to-all-done.2
  310.0 5.1 gather_fusion.6
  315.1 18.7 %all-to-all-done.8 = bf16[8,128,512]{2,1,0:T(8,128)(2,1)} async-done(((bf16[8,128,512]{2,1,0:T(8,128)(2,1)}), bf16[8,128,512]{2,1,0:T(8,128)(2,1)}, u32[]{:S(2)}, u32[]{:S(2)}) %all-to-all-start.8) | async-done | bytes 1048608 | tf_op jit(solution)/shard_map/all_to_all | solution.py:189
  344.8 5.1 gather_fusion.12
  349.9 13.5 %all-to-all-done.6 = bf16[8,128,512]{2,1,0:T(8,128)(2,1)} async-done(((bf16[8,128,512]{2,1,0:T(8,128)(2,1)}), bf16[8,128,512]{2,1,0:T(8,128)(2,1)}, u32[]{:S(2)}, u32[]{:S(2)}) %all-to-all-start.6) | async-done | bytes 1048608 | tf_op jit(solution)/shard_map/all_to_all | solution.py:97
  368.7 9.9 multiply_convert_fusion.2
  378.6 6.2 fusion.134
  384.8 8.3 all-to-all-done.12
  397.7 9.7 fusion.13
  412.7 11.0 %all-to-all-done.3 = bf16[8,128,512]{2,1,0:T(8,128)(2,1)S(1)} async-done(((bf16[8,128,512]{2,1,0:T(8,128)(2,1)}), bf16[8,128,512]{2,1,0:T(8,128)(2,1)S(1)}, u32[]{:S(2)}, u32[]{:S(2)}) %all-to-all-start.3) | async-done | bytes 1048608 | tf_op jit(solution)/shard_map/all_to_all | solution.py:106
  443.6 10.1 all-to-all-done.9
  457.3 9.7 fusion.27
  472.3 10.8 %all-to-all-done.7 = bf16[8,128,512]{2,1,0:T(8,128)(2,1)S(1)} async-done(((bf16[8,128,512]{2,1,0:T(8,128)(2,1)}), bf16[8,128,512]{2,1,0:T(8,128)(2,1)S(1)}, u32[]{:S(2)}, u32[]{:S(2)}) %all-to-all-start.7) | async-done | bytes 1048608 | tf_op jit(solution)/shard_map/all_to_all | solution.py:106
  586.3 6.0 all-to-all-start.10
  602.0 5.1 gather_fusion.14
  610.2 7.3 all-to-all-done.10
  621.2 9.7 fusion.6
  636.4 10.6 %all-to-all-done.14 = bf16[8,128,512]{2,1,0:T(8,128)(2,1)S(1)} async-done(((bf16[8,128,512]{2,1,0:T(8,128)(2,1)}), bf16[8,128,512]{2,1,0:T(8,128)(2,1)S(1)}, u32[]{:S(2)}, u32[]{:S(2)}) %all-to-all-start.14) | async-done | bytes 1048608 | tf_op jit(solution)/shard_map/all_to_all | solution.py:189
  651.6 9.7 fusion.20
  666.6 11.0 %all-to-all-done.11 = bf16[8,128,512]{2,1,0:T(8,128)(2,1)S(1)} async-done(((bf16[8,128,512]{2,1,0:T(8,128)(2,1)}), bf16[8,128,512]{2,1,0:T(8,128)(2,1)S(1)}, u32[]{:S(2)}, u32[]{:S(2)}) %all-to-all-start.11) | async-done | bytes 1048608 | tf_op jit(solution)/shard_map/all_to_all | solution.py:198
  701.7 6.8 all-to-all-done.15
  771.0 5.1 fusion.344
  776.2 9.7 fusion.39
  834.6 17.8 %reduce-scatter.22.cloned.1.call-done = bf16[128,4]{1,0:T(8,128)(2,1)} async-done(((bf16[512,4]{1,0:T(8,128)(2,1)}), bf16[128,4]{1,0:T(8,128)(2,1)}) %reduce-scatter.22.cloned.1.call-update) | async-done | bytes 1040
  853.3 21.6 %all-reduce.16 = (bf16[2,2,128]{2,1,0:T(2,128)(2,1)S(1)}, bf16[2,2,128]{2,1,0:T(2,128)(2,1)S(1)}, bf16[2,128,8]{1,2,0:T(8,128)(2,1)S(1)}) all-reduce(bf16[2,2,128]{2,1,0:T(2,128)(2,1)S(1)} %copy.259, bf16[2,2,128]{2,1,0:T(2,128)(2,1)S(1)} %copy.261, bf16[2,128,8]{1,2,0:T(8,128)(2,1)S(1)} %copy.263), channel_id=1, replica_groups=mesh['expert'=8,'shard'=4] {'expert'}, use_global_device_ids=true, to_apply=%region_89.90 | all-reduce | flops 3072 | bytes 12288 | tf_op jit(solution)/shard_map/psum | solution.py:344
  876.7 22.7 %reduce-scatter.20.cloned.1.call-done = bf16[2,1,512,512]{3,2,1,0:T(8,128)(2,1)} async-done(((bf16[2,1,2048,512]{3,2,1,0:T(8,128)(2,1)}), bf16[2,1,512,512]{3,2,1,0:T(8,128)(2,1)}) %reduce-scatter.20.cloned.1.call-update) | async-done | bytes 1048592 | tf_op jit(solution)/shard_map/reduce_scatter | solution.py:339
  902.3 44.3 %reduce-scatter.18.cloned.1.call-done = bf16[2,1,128,2048]{3,2,1,0:T(8,128)(2,1)} async-done(((bf16[2,1,512,2048]{3,2,1,0:T(8,128)(2,1)}), bf16[2,1,128,2048]{3,2,1,0:T(8,128)(2,1)}) %reduce-scatter.18.cloned.1.call-update) | async-done | bytes 1048592 | tf_op jit(solution)/shard_map/reduce_scatter | solution.py:336
  949.3 79.0 %all-reduce.20.cloned.1.call-done = (bf16[2,128,1536]{2,1,0:T(8,128)(2,1)}, bf16[2,128,512]{2,1,0:T(8,128)(2,1)}) async-done(((bf16[2,128,1536]{2,1,0:T(8,128)(2,1)}, bf16[2,128,512]{2,1,0:T(8,128)(2,1)}), (bf16[2,128,1536]{2,1,0:T(8,128)(2,1)}, bf16[2,128,512]{2,1,0:T(8,128)(2,1)})) %all-reduce.20.cloned.1.call-update) | async-done | bytes 1048592 | tf_op jit(solution)/shard_map/psum | solution.py:346
  (963 shorter events, 495.0 us)
Async XLA Ops:
  7.2 34.5 %all-gather.21.cloned.1.call-start = ((), (), s32[]{:S(2)}) async-start(), calls=%async_computation.27 | async-start | bytes 1966080 | tf_op jit(solution)/shard_map/all_gather | solution.py:279
  9.5 132.4 %all-gather.23.cloned.1.call-start = ((), (), s32[]{:S(2)}) async-start(), calls=%async_computation.28 | async-start | bytes 2621440 | tf_op jit(solution)/shard_map/all_gather | solution.py:282
  11.8 137.6 %all-gather.25.cloned.1.call-start = ((), (), s32[]{:S(2)}) async-start(), calls=%async_computation.29 | async-start | bytes 2621440 | tf_op jit(solution)/shard_map/all_gather | solution.py:283
  13.2 49.3 %copy-start.184 = (f32[394]{0:T(512)}, f32[394]{0:T(512)S(1)}, u32[]{:S(2)}) copy-start(f32[394]{0:T(512)S(1)} %broadcast_multiply_fusion.7) | copy-start | bytes 4732
  20.2 42.3 %copy-start.211 = (f32[1,1,512]{2,1,0:T(1,128)}, f32[1,1,512]{2,1,0:T(1,128)S(1)}, u32[]{:S(2)}) copy-start(f32[1,1,512]{2,1,0:T(1,128)S(1)} %get-tuple-element.137) | copy-start | bytes 6148
  20.2 66.7 %copy-start.186 = (f32[1,1,512]{2,1,0:T(1,128)}, f32[1,1,512]{2,1,0:T(1,128)S(1)}, u32[]{:S(2)}) copy-start(f32[1,1,512]{2,1,0:T(1,128)S(1)} %get-tuple-element.136) | copy-start | bytes 6148
  25.8 36.8 %copy-start.246 = (f32[1,1,512]{2,1,0:T(1,128)}, f32[1,1,512]{2,1,0:T(1,128)S(1)}, u32[]{:S(2)}) copy-start(f32[1,1,512]{2,1,0:T(1,128)S(1)} %get-tuple-element.139) | copy-start | bytes 6148
  34.7 48.4 %copy-start.37 = (bf16[1,512,512]{2,1,0:T(8,128)(2,1)}, bf16[1,512,512]{2,1,0:T(8,128)(2,1)S(1)}, u32[]{:S(2)}) copy-start(bf16[1,512,512]{2,1,0:T(8,128)(2,1)S(1)} %all-gather.3) | copy-start | bytes 1572868
  41.7 45.6 %copy-start.175 = (s32[1024]{0:T(1024)}, s32[1024]{0:T(1024)S(1)}, u32[]{:S(2)}) copy-start(s32[1024]{0:T(1024)S(1)} %get-tuple-element.99) | copy-start | bytes 12292
  84.7 144.4 %copy-start.11 = (f32[394,512]{1,0:T(8,128)}, f32[394,512]{1,0:T(8,128)S(1)}, u32[]{:S(2)}) copy-start(f32[394,512]{1,0:T(8,128)S(1)} %get-tuple-element.151) | copy-start | bytes 2420740
  86.6 142.5 %copy-start.13 = (f32[394,512]{1,0:T(8,128)}, f32[394,512]{1,0:T(8,128)S(1)}, u32[]{:S(2)}) copy-start(f32[394,512]{1,0:T(8,128)S(1)} %get-tuple-element.147) | copy-start | bytes 2420740
  87.2 111.8 %copy-start.50 = (bf16[394,512]{1,0:T(8,128)(2,1)}, bf16[394,512]{1,0:T(8,128)(2,1)S(1)}, u32[]{:S(2)}) copy-start(bf16[394,512]{1,0:T(8,128)(2,1)S(1)} %get-tuple-element.113) | copy-start | bytes 1210372
  87.3 112.1 %copy-start.51 = (bf16[394,512]{1,0:T(8,128)(2,1)}, bf16[394,512]{1,0:T(8,128)(2,1)S(1)}, u32[]{:S(2)}) copy-start(bf16[394,512]{1,0:T(8,128)(2,1)S(1)} %get-tuple-element.112) | copy-start | bytes 1210372
  92.8 31.9 %all-to-all-start.4 = ((bf16[8,128,512]{2,1,0:T(8,128)(2,1)}), bf16[8,128,512]{2,1,0:T(8,128)(2,1)}, u32[]{:S(2)}, u32[]{:S(2)}) async-start(bf16[8,128,512]{2,1,0:T(8,128)(2,1)} %bitcast.478), calls=%async_computation.4 | async-start | bytes 2097152 | tf_op jit(solution)/shard_map/all_to_all | solution.py:97
  98.4 132.7 %all-gather.27.cloned.1.call-start = ((), (), s32[]{:S(2)}) async-start(), calls=%async_computation.30 | async-start | bytes 1966080 | tf_op jit(solution)/shard_map/all_gather | solution.py:279
  110.8 120.3 %copy-start.213 = (f32[1,1,512]{2,1,0:T(1,128)}, f32[1,1,512]{2,1,0:T(1,128)S(1)}, u32[]{:S(2)}) copy-start(f32[1,1,512]{2,1,0:T(1,128)S(1)} %get-tuple-element.133) | copy-start | bytes 6148
  110.8 156.5 %copy-start.195 = (f32[1,1,512]{2,1,0:T(1,128)}, f32[1,1,512]{2,1,0:T(1,128)S(1)}, u32[]{:S(2)}) copy-start(f32[1,1,512]{2,1,0:T(1,128)S(1)} %get-tuple-element.132) | copy-start | bytes 6148
  110.9 182.5 %copy-start.173 = (s32[1024]{0:T(1024)}, s32[1024]{0:T(1024)S(1)}, u32[]{:S(2)}) copy-start(s32[1024]{0:T(1024)S(1)} %get-tuple-element.96) | copy-start | bytes 12292
  124.7 32.4 %all-to-all-start = ((bf16[8,128,512]{2,1,0:T(8,128)(2,1)}), bf16[8,128,512]{2,1,0:T(8,128)(2,1)}, u32[]{:S(2)}, u32[]{:S(2)}) async-start(bf16[8,128,512]{2,1,0:T(8,128)(2,1)} %bitcast.482), calls=%async_computation | async-start | bytes 2097152 | tf_op jit(solution)/shard_map/all_to_all | solution.py:97
  141.8 89.3 %copy-start.248 = (f32[1,1,512]{2,1,0:T(1,128)}, f32[1,1,512]{2,1,0:T(1,128)S(1)}, u32[]{:S(2)}) copy-start(f32[1,1,512]{2,1,0:T(1,128)S(1)} %get-tuple-element.135) | copy-start | bytes 6148
  157.2 32.3 %all-to-all-start.5 = ((bf16[8,128,512]{2,1,0:T(8,128)(2,1)}), bf16[8,128,512]{2,1,0:T(8,128)(2,1)}, u32[]{:S(2)}, u32[]{:S(2)}) async-start(bf16[8,128,512]{2,1,0:T(8,128)(2,1)} %bitcast.496), calls=%async_computation.5 | async-start | bytes 2097152 | tf_op jit(solution)/shard_map/all_to_all | solution.py:106
  163.1 38.1 %copy-start.132 = (s32[1024]{0:T(1024)}, s32[1024]{0:T(1024)S(1)}, u32[]{:S(2)}) copy-start(s32[1024]{0:T(1024)S(1)} %pad_clamp_fusion) | copy-start | bytes 12292
  163.2 36.6 %copy-start.136 = (s32[394,2]{0,1:T(2,128)}, s32[394,2]{0,1:T(2,128)S(1)}, u32[]{:S(2)}) copy-start(s32[394,2]{0,1:T(2,128)S(1)} %get-tuple-element.101) | copy-start | bytes 9460
  163.2 128.4 %copy-start.140 = (s32[394,2]{0,1:T(2,128)}, s32[394,2]{0,1:T(2,128)S(1)}, u32[]{:S(2)}) copy-start(s32[394,2]{0,1:T(2,128)S(1)} %get-tuple-element.100) | copy-start | bytes 9460
  189.4 29.8 %all-to-all-start.1 = ((bf16[8,128,512]{2,1,0:T(8,128)(2,1)}), bf16[8,128,512]{2,1,0:T(8,128)(2,1)}, u32[]{:S(2)}, u32[]{:S(2)}) async-start(bf16[8,128,512]{2,1,0:T(8,128)(2,1)} %bitcast.494), calls=%async_computation.1 | async-start | bytes 2097152 | tf_op jit(solution)/shard_map/all_to_all | solution.py:106
  193.9 97.7 %copy-start.167 = (pred[2,394]{1,0:T(4,128)(4,1)}, pred[2,394]{1,0:T(4,128)(4,1)S(1)}, u32[]{:S(2)}) copy-start(pred[2,394]{1,0:T(4,128)(4,1)S(1)} %lt.146) | copy-start | bytes 2368
  274.4 29.7 %all-to-all-start.2 = ((bf16[8,128,512]{2,1,0:T(8,128)(2,1)}), bf16[8,128,512]{2,1,0:T(8,128)(2,1)}, u32[]{:S(2)}, u32[]{:S(2)}) async-start(bf16[8,128,512]{2,1,0:T(8,128)(2,1)} %bitcast.480), calls=%async_computation.2 | async-start | bytes 2097152 | tf_op jit(solution)/shard_map/all_to_all | solution.py:97
  278.6 90.1 %all-gather.29.cloned.1.call-start = ((), (), s32[]{:S(2)}) async-start(), calls=%async_computation.31 | async-start | bytes 2621440 | tf_op jit(solution)/shard_map/all_gather | solution.py:282
  304.1 29.6 %all-to-all-start.8 = ((bf16[8,128,512]{2,1,0:T(8,128)(2,1)}), bf16[8,128,512]{2,1,0:T(8,128)(2,1)}, u32[]{:S(2)}, u32[]{:S(2)}) async-start(bf16[8,128,512]{2,1,0:T(8,128)(2,1)} %bitcast.483), calls=%async_computation.8 | async-start | bytes 2097152 | tf_op jit(solution)/shard_map/all_to_all | solution.py:189
  308.3 70.3 %all-gather.31.cloned.1.call-start = ((), (), s32[]{:S(2)}) async-start(), calls=%async_computation.32 | async-start | bytes 2621440 | tf_op jit(solution)/shard_map/all_gather | solution.py:283
  333.7 29.6 %all-to-all-start.6 = ((bf16[8,128,512]{2,1,0:T(8,128)(2,1)}), bf16[8,128,512]{2,1,0:T(8,128)(2,1)}, u32[]{:S(2)}, u32[]{:S(2)}) async-start(bf16[8,128,512]{2,1,0:T(8,128)(2,1)} %bitcast.481), calls=%async_computation.6 | async-start | bytes 2097152 | tf_op jit(solution)/shard_map/all_to_all | solution.py:97
  363.4 29.7 %all-to-all-start.12 = ((bf16[8,128,512]{2,1,0:T(8,128)(2,1)}), bf16[8,128,512]{2,1,0:T(8,128)(2,1)S(1)}, u32[]{:S(2)}, u32[]{:S(2)}) async-start(bf16[8,128,512]{2,1,0:T(8,128)(2,1)} %bitcast.484), calls=%async_computation.12 | async-start | bytes 2097152 | tf_op jit(solution)/shard_map/all_to_all | solution.py:189
  394.1 29.6 %all-to-all-start.3 = ((bf16[8,128,512]{2,1,0:T(8,128)(2,1)}), bf16[8,128,512]{2,1,0:T(8,128)(2,1)S(1)}, u32[]{:S(2)}, u32[]{:S(2)}) async-start(bf16[8,128,512]{2,1,0:T(8,128)(2,1)} %bitcast.497), calls=%async_computation.3 | async-start | bytes 2097152 | tf_op jit(solution)/shard_map/all_to_all | solution.py:106
  423.7 30.0 %all-to-all-start.9 = ((bf16[8,128,512]{2,1,0:T(8,128)(2,1)}), bf16[8,128,512]{2,1,0:T(8,128)(2,1)}, u32[]{:S(2)}, u32[]{:S(2)}) async-start(bf16[8,128,512]{2,1,0:T(8,128)(2,1)} %bitcast.495), calls=%async_computation.9 | async-start | bytes 2097152 | tf_op jit(solution)/shard_map/all_to_all | solution.py:198
  453.7 29.4 %all-to-all-start.7 = ((bf16[8,128,512]{2,1,0:T(8,128)(2,1)}), bf16[8,128,512]{2,1,0:T(8,128)(2,1)S(1)}, u32[]{:S(2)}, u32[]{:S(2)}) async-start(bf16[8,128,512]{2,1,0:T(8,128)(2,1)} %bitcast.498), calls=%async_computation.7 | async-start | bytes 2097152 | tf_op jit(solution)/shard_map/all_to_all | solution.py:106
  483.1 34.0 %all-to-all-start.13 = ((bf16[8,128,512]{2,1,0:T(8,128)(2,1)}), bf16[8,128,512]{2,1,0:T(8,128)(2,1)}, u32[]{:S(2)}, u32[]{:S(2)}) async-start(bf16[8,128,512]{2,1,0:T(8,128)(2,1)} %bitcast.493), calls=%async_computation.13 | async-start | bytes 2097152 | tf_op jit(solution)/shard_map/all_to_all | solution.py:198
  586.3 31.2 %all-to-all-start.10 = ((bf16[8,128,512]{2,1,0:T(8,128)(2,1)}), bf16[8,128,512]{2,1,0:T(8,128)(2,1)}, u32[]{:S(2)}, u32[]{:S(2)}) async-start(bf16[8,128,512]{2,1,0:T(8,128)(2,1)} %bitcast.477), calls=%async_computation.10 | async-start | bytes 2097152 | tf_op jit(solution)/shard_map/all_to_all | solution.py:189
  617.5 29.5 %all-to-all-start.14 = ((bf16[8,128,512]{2,1,0:T(8,128)(2,1)}), bf16[8,128,512]{2,1,0:T(8,128)(2,1)S(1)}, u32[]{:S(2)}, u32[]{:S(2)}) async-start(bf16[8,128,512]{2,1,0:T(8,128)(2,1)} %bitcast.479), calls=%async_computation.14 | async-start | bytes 2097152 | tf_op jit(solution)/shard_map/all_to_all | solution.py:189
  648.0 29.6 %all-to-all-start.11 = ((bf16[8,128,512]{2,1,0:T(8,128)(2,1)}), bf16[8,128,512]{2,1,0:T(8,128)(2,1)S(1)}, u32[]{:S(2)}, u32[]{:S(2)}) async-start(bf16[8,128,512]{2,1,0:T(8,128)(2,1)} %bitcast.499), calls=%async_computation.11 | async-start | bytes 2097152 | tf_op jit(solution)/shard_map/all_to_all | solution.py:198
  678.5 30.0 %all-to-all-start.15 = ((bf16[8,128,512]{2,1,0:T(8,128)(2,1)}), bf16[8,128,512]{2,1,0:T(8,128)(2,1)}, u32[]{:S(2)}, u32[]{:S(2)}) async-start(bf16[8,128,512]{2,1,0:T(8,128)(2,1)} %bitcast.492), calls=%async_computation.15 | async-start | bytes 2097152 | tf_op jit(solution)/shard_map/all_to_all | solution.py:198
  682.9 143.7 %reduce-scatter.26.cloned.1.call-start = ((), (), s32[]{:S(2)}) async-start(), calls=%async_computation.35 | async-start | bytes 163840
  688.8 142.0 %reduce-scatter.16.cloned.1.call-start = ((), (), s32[]{:S(2)}) async-start(), calls=%async_computation.24 | async-start | bytes 1310720 | tf_op jit(solution)/shard_map/reduce_scatter | solution.py:330
  744.1 86.7 %reduce-scatter.14.cloned.1.call-start = ((), (), s32[]{:S(2)}) async-start(), calls=%async_computation.23 | async-start | bytes 3932160 | tf_op jit(solution)/shard_map/reduce_scatter | solution.py:327
  770.7 63.0 %reduce-scatter.24.cloned.1.call-start = ((), (), s32[]{:S(2)}) async-start(), calls=%async_computation.34 | async-start | bytes 163840
  799.1 53.3 %reduce-scatter.22.cloned.1.call-start = ((), (), s32[]{:S(2)}) async-start(), calls=%async_computation.33 | async-start | bytes 163840
  800.4 99.0 %reduce-scatter.20.cloned.1.call-start = ((), (), s32[]{:S(2)}) async-start(), calls=%async_computation.26 | async-start | bytes 5242880 | tf_op jit(solution)/shard_map/reduce_scatter | solution.py:339
  805.1 141.4 %reduce-scatter.18.cloned.1.call-start = ((), (), s32[]{:S(2)}) async-start(), calls=%async_computation.25 | async-start | bytes 5242880 | tf_op jit(solution)/shard_map/reduce_scatter | solution.py:336
  823.9 204.4 %all-reduce.20.cloned.1.call-start = ((), (), s32[]{:S(2)}) async-start(), calls=%async_computation.36 | async-start | bytes 2097152 | tf_op jit(solution)/shard_map/psum | solution.py:346
  (264 other events, 1439.7 us)
Sparse Core Ops, SparseCore 0:
  10.1 23.2 all-gather.20
  35.6 21.9 all-gather.22
  59.8 22.5 all-gather.24
  100.4 20.5 all-gather.26
  280.7 23.2 all-gather.28
  310.4 23.2 all-gather.30
  688.9 20.3 reduce-scatter.25
  744.2 23.0 reduce-scatter.15
  770.9 36.8 reduce-scatter.13
  810.1 19.6 reduce-scatter.23
  832.7 19.6 reduce-scatter.21
  854.8 44.5 reduce-scatter.19
  901.9 44.5 reduce-scatter.17
  949.9 78.2 all-reduce.19
where the time goes:
time: 1050 us; the launch traced here: 1040 us
  waiting for transfers between devices  311 us (30%)
  local copies, waits for them, and re-layouts  258 us (25%)
  matrix products  229 us (22%)
  other arithmetic  82.1 us (8%)
  starting transfers between devices  71.9 us (7%)
  blocking collectives  69.1 us (7%)
  between operations  18.1 us (2%)
    psum x1, waiting for transfers between devices, local(): lax.psum(scattered[2].astype(jnp.bfloat16), 'expert').astype(jnp.float32)  79 us
    dot_general x20, matrix products, dot_last(): lax.dot_general(left, right, (((1,), (1,)), ((), ())), preferred_element_...  70.6 us
    dot_general x20, matrix products, dot_first(): lax.dot_general(left, right, (((0,), (0,)), ((), ())), preferred_element_...  57.3 us
    unnamed x588, local copies, waits for them, and re-layouts  53.8 us
    all_to_all x4, waiting for transfers between devices, forward_layer(): lax.all_to_all(expert_rows.reshape(sources, item_count, D), 'expert', spl...  45.3 us
    all_to_all x4, waiting for transfers between devices, backward_layer(): lax.all_to_all(d_slots, 'expert', split_axis=0, concat_axis=0, tiled=True)  45 us
    reduce_scatter x1, waiting for transfers between devices, local(): lax.psum_scatter(stacked[5].astype(jnp.bfloat16), 'shard', scatter_dimens...  44.3 us
    dot_general x4, matrix products, forward_layer(): hidden_pre = jnp.dot(row_block, in_w[0], preferred_element_type=jnp.float32)  30.8 us
  transfers between devices with their start and end apart: 30, of which 18 were waited for; matrix products, arithmetic and copies ran while one was open for 41% of the time, Pallas kernels for 0%

commit v1 on v0

--- a/solution.py
+++ b/solution.py
@@ -341,7 +341,9 @@
         ).astype(jnp.float32),
     )
     replicated = (
-        lax.psum(scattered[0].astype(jnp.bfloat16), "expert").astype(jnp.float32),
+        jnp.sum(lax.all_gather(scattered[0].astype(jnp.bfloat16), "expert"), axis=0).astype(
+            jnp.float32
+        ),
         lax.psum(scattered[1].astype(jnp.bfloat16), "expert").astype(jnp.float32),
         lax.psum(scattered[2].astype(jnp.bfloat16), "expert").astype(jnp.float32),
         lax.psum(scattered[3].astype(jnp.bfloat16), "expert").astype(jnp.float32),

time: 1050 us -> 1050 us (level)
  blocking collectives: 69.1 us -> 84.6 us
  waiting for transfers between devices: 311 us -> 296 us
    unnamed x17, waiting for transfers between devices: 19.5 us -> 1.76 us
    all_gather x0 -> x1, blocking collectives: none -> 17.6 us  [local(): lax.all_gather(scattered[0].astype(jnp.bfloat16), 'expert')]
  transfers between devices with their start and end apart: 30 -> 30, of which waited for: 18 -> 17; matrix products, arithmetic and copies ran while one was open for 41% -> 41% of each run, Pallas kernels for 0% -> 0%
where the time goes in v1:
time: 1050 us; the launch traced here: 1040 us
  waiting for transfers between devices  296 us (28%)
  local copies, waits for them, and re-layouts  258 us (25%)
  matrix products  229 us (22%)
  blocking collectives  84.6 us (8%)
  other arithmetic  82.1 us (8%)
  starting transfers between devices  71.9 us (7%)
  between operations  18.1 us (2%)
    psum x1, waiting for transfers between devices, local(): lax.psum(scattered[2].astype(jnp.bfloat16), 'expert').astype(jnp.float32)  79 us
    dot_general x20, matrix products, dot_last(): lax.dot_general(left, right, (((1,), (1,)), ((), ())), preferred_element_...  70.6 us
    dot_general x20, matrix products, dot_first(): lax.dot_general(left, right, (((0,), (0,)), ((), ())), preferred_element_...  57.3 us
    unnamed x588, local copies, waits for them, and re-layouts  53.8 us
    all_to_all x4, waiting for transfers between devices, forward_layer(): lax.all_to_all(expert_rows.reshape(sources, item_count, D), 'expert', spl...  45.3 us
    all_to_all x4, waiting for transfers between devices, backward_layer(): lax.all_to_all(d_slots, 'expert', split_axis=0, concat_axis=0, tiled=True)  45 us
    reduce_scatter x1, waiting for transfers between devices, local(): lax.psum_scatter(stacked[5].astype(jnp.bfloat16), 'shard', scatter_dimens...  44.3 us
    dot_general x4, matrix products, forward_layer(): hidden_pre = jnp.dot(row_block, in_w[0], preferred_element_type=jnp.float32)  30.7 us
  transfers between devices with their start and end apart: 30, of which 17 were waited for; matrix products, arithmetic and copies ran while one was open for 41% of the time, Pallas kernels for 0%

profile of v1, /device:TPU:0, one launch (start us, length us, event | category | flops | bytes accessed | tf_op | source)
XLA Modules:
  0.0 1039.4 jit_solution(13648900708640493041)
XLA Ops:
  14.2 6.0 all-gather
  20.3 5.5 all-gather.1
  26.5 8.2 all-gather.3
  35.8 5.3 scatter_custom_fusion.1
  87.3 5.5 gather_fusion.4
  92.8 5.5 all-to-all-start.4
  99.8 5.3 scatter_custom_fusion
  110.9 5.1 gather_fusion
  116.0 8.8 all-to-all-done.4
  129.0 7.2 all-gather.10
  141.8 7.6 fusion.80
  149.4 7.7 fusion.125
  157.2 5.9 all-to-all-start.5
  163.1 8.9 multiply_convert_fusion.3
  177.4 12.0 %all-to-all-done.5 = bf16[8,128,512]{2,1,0:T(8,128)(2,1)} async-done(((bf16[8,128,512]{2,1,0:T(8,128)(2,1)}), bf16[8,128,512]{2,1,0:T(8,128)(2,1)}, u32[]{:S(2)}, u32[]{:S(2)}) %all-to-all-start.5) | async-done | bytes 1048608 | tf_op jit(solution)/shard_map/all_to_all | solution.py:106
  193.9 5.2 all-gather.4
  207.8 11.5 %all-to-all-done.1 = bf16[8,128,512]{2,1,0:T(8,128)(2,1)} async-done(((bf16[8,128,512]{2,1,0:T(8,128)(2,1)}), bf16[8,128,512]{2,1,0:T(8,128)(2,1)}, u32[]{:S(2)}, u32[]{:S(2)}) %all-to-all-start.1) | async-done | bytes 1048608 | tf_op jit(solution)/shard_map/all_to_all | solution.py:106
  269.3 5.1 gather_fusion.2
  285.1 5.2 all-gather.11
  293.4 5.1 gather_fusion.8
  298.5 5.6 all-to-all-done.2
  310.0 5.1 gather_fusion.6
  315.1 18.7 %all-to-all-done.8 = bf16[8,128,512]{2,1,0:T(8,128)(2,1)} async-done(((bf16[8,128,512]{2,1,0:T(8,128)(2,1)}), bf16[8,128,512]{2,1,0:T(8,128)(2,1)}, u32[]{:S(2)}, u32[]{:S(2)}) %all-to-all-start.8) | async-done | bytes 1048608 | tf_op jit(solution)/shard_map/all_to_all | solution.py:189
  344.9 5.1 gather_fusion.12
  350.0 13.5 %all-to-all-done.6 = bf16[8,128,512]{2,1,0:T(8,128)(2,1)} async-done(((bf16[8,128,512]{2,1,0:T(8,128)(2,1)}), bf16[8,128,512]{2,1,0:T(8,128)(2,1)}, u32[]{:S(2)}, u32[]{:S(2)}) %all-to-all-start.6) | async-done | bytes 1048608 | tf_op jit(solution)/shard_map/all_to_all | solution.py:97
  368.7 9.9 multiply_convert_fusion.2
  378.6 6.2 fusion.134
  384.8 8.4 all-to-all-done.12
  397.8 9.7 fusion.13
  412.8 11.0 %all-to-all-done.3 = bf16[8,128,512]{2,1,0:T(8,128)(2,1)S(1)} async-done(((bf16[8,128,512]{2,1,0:T(8,128)(2,1)}), bf16[8,128,512]{2,1,0:T(8,128)(2,1)S(1)}, u32[]{:S(2)}, u32[]{:S(2)}) %all-to-all-start.3) | async-done | bytes 1048608 | tf_op jit(solution)/shard_map/all_to_all | solution.py:106
  443.7 10.1 all-to-all-done.9
  457.3 9.7 fusion.27
  472.3 10.8 %all-to-all-done.7 = bf16[8,128,512]{2,1,0:T(8,128)(2,1)S(1)} async-done(((bf16[8,128,512]{2,1,0:T(8,128)(2,1)}), bf16[8,128,512]{2,1,0:T(8,128)(2,1)S(1)}, u32[]{:S(2)}, u32[]{:S(2)}) %all-to-all-start.7) | async-done | bytes 1048608 | tf_op jit(solution)/shard_map/all_to_all | solution.py:106
  581.3 5.1 gather_fusion.10
  586.4 6.0 all-to-all-start.10
  602.1 5.1 gather_fusion.14
  610.3 7.3 all-to-all-done.10
  621.3 9.7 fusion.6
  636.4 10.6 %all-to-all-done.14 = bf16[8,128,512]{2,1,0:T(8,128)(2,1)S(1)} async-done(((bf16[8,128,512]{2,1,0:T(8,128)(2,1)}), bf16[8,128,512]{2,1,0:T(8,128)(2,1)S(1)}, u32[]{:S(2)}, u32[]{:S(2)}) %all-to-all-start.14) | async-done | bytes 1048608 | tf_op jit(solution)/shard_map/all_to_all | solution.py:189
  651.7 9.7 fusion.20
  666.6 11.0 %all-to-all-done.11 = bf16[8,128,512]{2,1,0:T(8,128)(2,1)S(1)} async-done(((bf16[8,128,512]{2,1,0:T(8,128)(2,1)}), bf16[8,128,512]{2,1,0:T(8,128)(2,1)S(1)}, u32[]{:S(2)}, u32[]{:S(2)}) %all-to-all-start.11) | async-done | bytes 1048608 | tf_op jit(solution)/shard_map/all_to_all | solution.py:198
  701.7 6.8 all-to-all-done.15
  776.3 9.7 fusion.39
  834.7 19.5 %all-reduce.16 = (bf16[2,2,128]{2,1,0:T(2,128)(2,1)S(1)}, bf16[2,128,8]{1,2,0:T(8,128)(2,1)S(1)}) all-reduce(bf16[2,2,128]{2,1,0:T(2,128)(2,1)S(1)} %copy.261, bf16[2,128,8]{1,2,0:T(8,128)(2,1)S(1)} %copy.263), channel_id=1, replica_groups=mesh['expert'=8,'shard'=4] {'expert'}, use_global_device_ids=true, to_apply=%region_99.100 | all-reduce | flops 2560 | bytes 10240 | tf_op jit(solution)/shard_map/psum | solution.py:347
  856.4 17.6 %all-gather.14 = bf16[16,2,128]{2,1,0:T(2,128)(2,1)S(1)} all-gather(bf16[2,2,128]{2,1,0:T(2,128)(2,1)S(1)} %copy.259), channel_id=16, replica_groups=mesh['expert'=8,'shard'=4] {'expert'}, dimensions={0}, use_global_device_ids=true | all-gather | bytes 9216 | tf_op jit(solution)/shard_map/all_gather | solution.py:344
  874.6 24.9 %reduce-scatter.20.cloned.1.call-done = bf16[2,1,512,512]{3,2,1,0:T(8,128)(2,1)} async-done(((bf16[2,1,2048,512]{3,2,1,0:T(8,128)(2,1)}), bf16[2,1,512,512]{3,2,1,0:T(8,128)(2,1)}) %reduce-scatter.20.cloned.1.call-update) | async-done | bytes 1048592 | tf_op jit(solution)/shard_map/reduce_scatter | solution.py:339
  902.3 44.3 %reduce-scatter.18.cloned.1.call-done = bf16[2,1,128,2048]{3,2,1,0:T(8,128)(2,1)} async-done(((bf16[2,1,512,2048]{3,2,1,0:T(8,128)(2,1)}), bf16[2,1,128,2048]{3,2,1,0:T(8,128)(2,1)}) %reduce-scatter.18.cloned.1.call-update) | async-done | bytes 1048592 | tf_op jit(solution)/shard_map/reduce_scatter | solution.py:336
  949.4 79.0 %all-reduce.20.cloned.1.call-done = (bf16[2,128,1536]{2,1,0:T(8,128)(2,1)}, bf16[2,128,512]{2,1,0:T(8,128)(2,1)}) async-done(((bf16[2,128,1536]{2,1,0:T(8,128)(2,1)}, bf16[2,128,512]{2,1,0:T(8,128)(2,1)}), (bf16[2,128,1536]{2,1,0:T(8,128)(2,1)}, bf16[2,128,512]{2,1,0:T(8,128)(2,1)})) %all-reduce.20.cloned.1.call-update) | async-done | bytes 1048592 | tf_op jit(solution)/shard_map/psum | solution.py:348
  (965 shorter events, 495.0 us)
Async XLA Ops:
  7.2 34.5 %all-gather.22.cloned.1.call-start = ((), (), s32[]{:S(2)}) async-start(), calls=%async_computation.27 | async-start | bytes 1966080 | tf_op jit(solution)/shard_map/all_gather | solution.py:279
  9.5 132.4 %all-gather.24.cloned.1.call-start = ((), (), s32[]{:S(2)}) async-start(), calls=%async_computation.28 | async-start | bytes 2621440 | tf_op jit(solution)/shard_map/all_gather | solution.py:282
  11.8 137.6 %all-gather.26.cloned.1.call-start = ((), (), s32[]{:S(2)}) async-start(), calls=%async_computation.29 | async-start | bytes 2621440 | tf_op jit(solution)/shard_map/all_gather | solution.py:283
  13.2 49.3 %copy-start.184 = (f32[394]{0:T(512)}, f32[394]{0:T(512)S(1)}, u32[]{:S(2)}) copy-start(f32[394]{0:T(512)S(1)} %broadcast_multiply_fusion.7) | copy-start | bytes 4732
  20.2 42.3 %copy-start.211 = (f32[1,1,512]{2,1,0:T(1,128)}, f32[1,1,512]{2,1,0:T(1,128)S(1)}, u32[]{:S(2)}) copy-start(f32[1,1,512]{2,1,0:T(1,128)S(1)} %get-tuple-element.136) | copy-start | bytes 6148
  20.2 66.6 %copy-start.186 = (f32[1,1,512]{2,1,0:T(1,128)}, f32[1,1,512]{2,1,0:T(1,128)S(1)}, u32[]{:S(2)}) copy-start(f32[1,1,512]{2,1,0:T(1,128)S(1)} %get-tuple-element.135) | copy-start | bytes 6148
  25.8 36.7 %copy-start.246 = (f32[1,1,512]{2,1,0:T(1,128)}, f32[1,1,512]{2,1,0:T(1,128)S(1)}, u32[]{:S(2)}) copy-start(f32[1,1,512]{2,1,0:T(1,128)S(1)} %get-tuple-element.138) | copy-start | bytes 6148
  34.7 48.3 %copy-start.37 = (bf16[1,512,512]{2,1,0:T(8,128)(2,1)}, bf16[1,512,512]{2,1,0:T(8,128)(2,1)S(1)}, u32[]{:S(2)}) copy-start(bf16[1,512,512]{2,1,0:T(8,128)(2,1)S(1)} %all-gather.3) | copy-start | bytes 1572868
  41.7 45.6 %copy-start.175 = (s32[1024]{0:T(1024)}, s32[1024]{0:T(1024)S(1)}, u32[]{:S(2)}) copy-start(s32[1024]{0:T(1024)S(1)} %get-tuple-element.98) | copy-start | bytes 12292
  84.7 144.4 %copy-start.11 = (f32[394,512]{1,0:T(8,128)}, f32[394,512]{1,0:T(8,128)S(1)}, u32[]{:S(2)}) copy-start(f32[394,512]{1,0:T(8,128)S(1)} %get-tuple-element.150) | copy-start | bytes 2420740
  86.5 142.6 %copy-start.13 = (f32[394,512]{1,0:T(8,128)}, f32[394,512]{1,0:T(8,128)S(1)}, u32[]{:S(2)}) copy-start(f32[394,512]{1,0:T(8,128)S(1)} %get-tuple-element.146) | copy-start | bytes 2420740
  87.2 111.8 %copy-start.50 = (bf16[394,512]{1,0:T(8,128)(2,1)}, bf16[394,512]{1,0:T(8,128)(2,1)S(1)}, u32[]{:S(2)}) copy-start(bf16[394,512]{1,0:T(8,128)(2,1)S(1)} %get-tuple-element.112) | copy-start | bytes 1210372
  87.2 112.1 %copy-start.51 = (bf16[394,512]{1,0:T(8,128)(2,1)}, bf16[394,512]{1,0:T(8,128)(2,1)S(1)}, u32[]{:S(2)}) copy-start(bf16[394,512]{1,0:T(8,128)(2,1)S(1)} %get-tuple-element.111) | copy-start | bytes 1210372
  92.8 31.9 %all-to-all-start.4 = ((bf16[8,128,512]{2,1,0:T(8,128)(2,1)}), bf16[8,128,512]{2,1,0:T(8,128)(2,1)}, u32[]{:S(2)}, u32[]{:S(2)}) async-start(bf16[8,128,512]{2,1,0:T(8,128)(2,1)} %bitcast.479), calls=%async_computation.4 | async-start | bytes 2097152 | tf_op jit(solution)/shard_map/all_to_all | solution.py:97
  98.3 132.8 %all-gather.28.cloned.1.call-start = ((), (), s32[]{:S(2)}) async-start(), calls=%async_computation.30 | async-start | bytes 1966080 | tf_op jit(solution)/shard_map/all_gather | solution.py:279
  110.8 120.4 %copy-start.213 = (f32[1,1,512]{2,1,0:T(1,128)}, f32[1,1,512]{2,1,0:T(1,128)S(1)}, u32[]{:S(2)}) copy-start(f32[1,1,512]{2,1,0:T(1,128)S(1)} %get-tuple-element.132) | copy-start | bytes 6148
  110.8 156.6 %copy-start.195 = (f32[1,1,512]{2,1,0:T(1,128)}, f32[1,1,512]{2,1,0:T(1,128)S(1)}, u32[]{:S(2)}) copy-start(f32[1,1,512]{2,1,0:T(1,128)S(1)} %get-tuple-element.131) | copy-start | bytes 6148
  110.8 182.6 %copy-start.173 = (s32[1024]{0:T(1024)}, s32[1024]{0:T(1024)S(1)}, u32[]{:S(2)}) copy-start(s32[1024]{0:T(1024)S(1)} %get-tuple-element.95) | copy-start | bytes 12292
  124.7 32.4 %all-to-all-start = ((bf16[8,128,512]{2,1,0:T(8,128)(2,1)}), bf16[8,128,512]{2,1,0:T(8,128)(2,1)}, u32[]{:S(2)}, u32[]{:S(2)}) async-start(bf16[8,128,512]{2,1,0:T(8,128)(2,1)} %bitcast.483), calls=%async_computation | async-start | bytes 2097152 | tf_op jit(solution)/shard_map/all_to_all | solution.py:97
  141.8 89.3 %copy-start.248 = (f32[1,1,512]{2,1,0:T(1,128)}, f32[1,1,512]{2,1,0:T(1,128)S(1)}, u32[]{:S(2)}) copy-start(f32[1,1,512]{2,1,0:T(1,128)S(1)} %get-tuple-element.134) | copy-start | bytes 6148
  157.2 32.3 %all-to-all-start.5 = ((bf16[8,128,512]{2,1,0:T(8,128)(2,1)}), bf16[8,128,512]{2,1,0:T(8,128)(2,1)}, u32[]{:S(2)}, u32[]{:S(2)}) async-start(bf16[8,128,512]{2,1,0:T(8,128)(2,1)} %bitcast.497), calls=%async_computation.5 | async-start | bytes 2097152 | tf_op jit(solution)/shard_map/all_to_all | solution.py:106
  163.1 38.1 %copy-start.132 = (s32[1024]{0:T(1024)}, s32[1024]{0:T(1024)S(1)}, u32[]{:S(2)}) copy-start(s32[1024]{0:T(1024)S(1)} %pad_clamp_fusion) | copy-start | bytes 12292
  163.1 36.6 %copy-start.136 = (s32[394,2]{0,1:T(2,128)}, s32[394,2]{0,1:T(2,128)S(1)}, u32[]{:S(2)}) copy-start(s32[394,2]{0,1:T(2,128)S(1)} %get-tuple-element.100) | copy-start | bytes 9460
  163.1 128.5 %copy-start.140 = (s32[394,2]{0,1:T(2,128)}, s32[394,2]{0,1:T(2,128)S(1)}, u32[]{:S(2)}) copy-start(s32[394,2]{0,1:T(2,128)S(1)} %get-tuple-element.99) | copy-start | bytes 9460
  189.4 29.9 %all-to-all-start.1 = ((bf16[8,128,512]{2,1,0:T(8,128)(2,1)}), bf16[8,128,512]{2,1,0:T(8,128)(2,1)}, u32[]{:S(2)}, u32[]{:S(2)}) async-start(bf16[8,128,512]{2,1,0:T(8,128)(2,1)} %bitcast.495), calls=%async_computation.1 | async-start | bytes 2097152 | tf_op jit(solution)/shard_map/all_to_all | solution.py:106
  193.9 97.8 %copy-start.167 = (pred[2,394]{1,0:T(4,128)(4,1)}, pred[2,394]{1,0:T(4,128)(4,1)S(1)}, u32[]{:S(2)}) copy-start(pred[2,394]{1,0:T(4,128)(4,1)S(1)} %lt.146) | copy-start | bytes 2368
  274.4 29.7 %all-to-all-start.2 = ((bf16[8,128,512]{2,1,0:T(8,128)(2,1)}), bf16[8,128,512]{2,1,0:T(8,128)(2,1)}, u32[]{:S(2)}, u32[]{:S(2)}) async-start(bf16[8,128,512]{2,1,0:T(8,128)(2,1)} %bitcast.481), calls=%async_computation.2 | async-start | bytes 2097152 | tf_op jit(solution)/shard_map/all_to_all | solution.py:97
  278.7 90.1 %all-gather.30.cloned.1.call-start = ((), (), s32[]{:S(2)}) async-start(), calls=%async_computation.31 | async-start | bytes 2621440 | tf_op jit(solution)/shard_map/all_gather | solution.py:282
  304.1 29.6 %all-to-all-start.8 = ((bf16[8,128,512]{2,1,0:T(8,128)(2,1)}), bf16[8,128,512]{2,1,0:T(8,128)(2,1)}, u32[]{:S(2)}, u32[]{:S(2)}) async-start(bf16[8,128,512]{2,1,0:T(8,128)(2,1)} %bitcast.484), calls=%async_computation.8 | async-start | bytes 2097152 | tf_op jit(solution)/shard_map/all_to_all | solution.py:189
  308.4 70.2 %all-gather.32.cloned.1.call-start = ((), (), s32[]{:S(2)}) async-start(), calls=%async_computation.32 | async-start | bytes 2621440 | tf_op jit(solution)/shard_map/all_gather | solution.py:283
  333.8 29.6 %all-to-all-start.6 = ((bf16[8,128,512]{2,1,0:T(8,128)(2,1)}), bf16[8,128,512]{2,1,0:T(8,128)(2,1)}, u32[]{:S(2)}, u32[]{:S(2)}) async-start(bf16[8,128,512]{2,1,0:T(8,128)(2,1)} %bitcast.482), calls=%async_computation.6 | async-start | bytes 2097152 | tf_op jit(solution)/shard_map/all_to_all | solution.py:97
  363.4 29.7 %all-to-all-start.12 = ((bf16[8,128,512]{2,1,0:T(8,128)(2,1)}), bf16[8,128,512]{2,1,0:T(8,128)(2,1)S(1)}, u32[]{:S(2)}, u32[]{:S(2)}) async-start(bf16[8,128,512]{2,1,0:T(8,128)(2,1)} %bitcast.485), calls=%async_computation.12 | async-start | bytes 2097152 | tf_op jit(solution)/shard_map/all_to_all | solution.py:189
  394.2 29.6 %all-to-all-start.3 = ((bf16[8,128,512]{2,1,0:T(8,128)(2,1)}), bf16[8,128,512]{2,1,0:T(8,128)(2,1)S(1)}, u32[]{:S(2)}, u32[]{:S(2)}) async-start(bf16[8,128,512]{2,1,0:T(8,128)(2,1)} %bitcast.498), calls=%async_computation.3 | async-start | bytes 2097152 | tf_op jit(solution)/shard_map/all_to_all | solution.py:106
  423.7 30.0 %all-to-all-start.9 = ((bf16[8,128,512]{2,1,0:T(8,128)(2,1)}), bf16[8,128,512]{2,1,0:T(8,128)(2,1)}, u32[]{:S(2)}, u32[]{:S(2)}) async-start(bf16[8,128,512]{2,1,0:T(8,128)(2,1)} %bitcast.496), calls=%async_computation.9 | async-start | bytes 2097152 | tf_op jit(solution)/shard_map/all_to_all | solution.py:198
  453.8 29.4 %all-to-all-start.7 = ((bf16[8,128,512]{2,1,0:T(8,128)(2,1)}), bf16[8,128,512]{2,1,0:T(8,128)(2,1)S(1)}, u32[]{:S(2)}, u32[]{:S(2)}) async-start(bf16[8,128,512]{2,1,0:T(8,128)(2,1)} %bitcast.499), calls=%async_computation.7 | async-start | bytes 2097152 | tf_op jit(solution)/shard_map/all_to_all | solution.py:106
  483.1 34.0 %all-to-all-start.13 = ((bf16[8,128,512]{2,1,0:T(8,128)(2,1)}), bf16[8,128,512]{2,1,0:T(8,128)(2,1)}, u32[]{:S(2)}, u32[]{:S(2)}) async-start(bf16[8,128,512]{2,1,0:T(8,128)(2,1)} %bitcast.494), calls=%async_computation.13 | async-start | bytes 2097152 | tf_op jit(solution)/shard_map/all_to_all | solution.py:198
  586.4 31.1 %all-to-all-start.10 = ((bf16[8,128,512]{2,1,0:T(8,128)(2,1)}), bf16[8,128,512]{2,1,0:T(8,128)(2,1)}, u32[]{:S(2)}, u32[]{:S(2)}) async-start(bf16[8,128,512]{2,1,0:T(8,128)(2,1)} %bitcast.478), calls=%async_computation.10 | async-start | bytes 2097152 | tf_op jit(solution)/shard_map/all_to_all | solution.py:189
  617.6 29.5 %all-to-all-start.14 = ((bf16[8,128,512]{2,1,0:T(8,128)(2,1)}), bf16[8,128,512]{2,1,0:T(8,128)(2,1)S(1)}, u32[]{:S(2)}, u32[]{:S(2)}) async-start(bf16[8,128,512]{2,1,0:T(8,128)(2,1)} %bitcast.480), calls=%async_computation.14 | async-start | bytes 2097152 | tf_op jit(solution)/shard_map/all_to_all | solution.py:189
  648.0 29.6 %all-to-all-start.11 = ((bf16[8,128,512]{2,1,0:T(8,128)(2,1)}), bf16[8,128,512]{2,1,0:T(8,128)(2,1)S(1)}, u32[]{:S(2)}, u32[]{:S(2)}) async-start(bf16[8,128,512]{2,1,0:T(8,128)(2,1)} %bitcast.500), calls=%async_computation.11 | async-start | bytes 2097152 | tf_op jit(solution)/shard_map/all_to_all | solution.py:198
  678.6 30.0 %all-to-all-start.15 = ((bf16[8,128,512]{2,1,0:T(8,128)(2,1)}), bf16[8,128,512]{2,1,0:T(8,128)(2,1)}, u32[]{:S(2)}, u32[]{:S(2)}) async-start(bf16[8,128,512]{2,1,0:T(8,128)(2,1)} %bitcast.493), calls=%async_computation.15 | async-start | bytes 2097152 | tf_op jit(solution)/shard_map/all_to_all | solution.py:198
  682.9 143.7 %reduce-scatter.26.cloned.1.call-start = ((), (), s32[]{:S(2)}) async-start(), calls=%async_computation.35 | async-start | bytes 163840
  688.8 142.0 %reduce-scatter.16.cloned.1.call-start = ((), (), s32[]{:S(2)}) async-start(), calls=%async_computation.24 | async-start | bytes 1310720 | tf_op jit(solution)/shard_map/reduce_scatter | solution.py:330
  744.1 86.7 %reduce-scatter.14.cloned.1.call-start = ((), (), s32[]{:S(2)}) async-start(), calls=%async_computation.23 | async-start | bytes 3932160 | tf_op jit(solution)/shard_map/reduce_scatter | solution.py:327
  770.8 63.0 %reduce-scatter.24.cloned.1.call-start = ((), (), s32[]{:S(2)}) async-start(), calls=%async_computation.34 | async-start | bytes 163840
  799.2 56.3 %reduce-scatter.22.cloned.1.call-start = ((), (), s32[]{:S(2)}) async-start(), calls=%async_computation.33 | async-start | bytes 163840
  800.5 99.0 %reduce-scatter.20.cloned.1.call-start = ((), (), s32[]{:S(2)}) async-start(), calls=%async_computation.26 | async-start | bytes 5242880 | tf_op jit(solution)/shard_map/reduce_scatter | solution.py:339
  805.2 141.4 %reduce-scatter.18.cloned.1.call-start = ((), (), s32[]{:S(2)}) async-start(), calls=%async_computation.25 | async-start | bytes 5242880 | tf_op jit(solution)/shard_map/reduce_scatter | solution.py:336
  823.9 204.5 %all-reduce.20.cloned.1.call-start = ((), (), s32[]{:S(2)}) async-start(), calls=%async_computation.36 | async-start | bytes 2097152 | tf_op jit(solution)/shard_map/psum | solution.py:348
  (264 other events, 1439.5 us)
Sparse Core Ops, SparseCore 0:
  10.1 23.2 all-gather.21
  35.6 21.9 all-gather.23
  59.8 22.5 all-gather.25
  100.4 20.5 all-gather.27
  280.7 23.3 all-gather.29
  310.4 23.2 all-gather.31
  689.0 20.3 reduce-scatter.25
  744.3 23.0 reduce-scatter.15
  770.9 36.8 reduce-scatter.13
  810.1 19.6 reduce-scatter.23
  832.8 19.6 reduce-scatter.21
  854.9 44.5 reduce-scatter.19
  902.0 44.5 reduce-scatter.17
  950.0 78.3 all-reduce.19
